TPU v7x, 256 devices: a whole 4x4x8 slice. The times are simulated.
256 devices in a mesh: req: 64 (over y, z_lo, x, core), tp: 4 (over z_hi).
Axes of the slice: x: 4, y: 4, z: 8 (z_hi: 4, z_lo: 2; z = z_hi * 2 + z_lo), core: 2. Of those that a mesh axis runs over, the one named last changes fastest.
Arguments:
- tokens: bfloat16 [16384, 2048], P('req'), may hold values from -6 to 6
- norm_gain: float32 [2048], replicated, may hold values from 0.25 to 1.75
- w_query: bfloat16 [2048, 2048], P(None, 'tp'), may hold values from -1 to 1
- w_key: bfloat16 [2048, 2048], P(None, 'tp'), may hold values from -1 to 1
- w_value: bfloat16 [2048, 2048], P(None, 'tp'), may hold values from -0.125 to 0.125
- w_out: bfloat16 [2048, 2048], P('tp'), may hold values from -0.125 to 0.125
- lambdas: float32 [4, 8, 128], P(None, 'tp'), may hold values from -1 to 1
- sub_gain: float32 [8, 256], P('tp'), may hold values from 0.5 to 2
- lengths: int32 [4], replicated, may hold values from 1 to 8192, 16384 in all
Outputs:
- hidden: bfloat16 [16384, 2048], P('req')
- key_cache: bfloat16 [16384, 2048], P('req', 'tp')
- value_cache: bfloat16 [16384, 2048], P('req', 'tp')
Inputs may be any that keep to these rules, and one draw needn't show every extreme that they name: The lengths sum to 16384; the longest is exactly 8192.
All inputs are finite; a program needn't handle non-finite values.
Results may differ from a plain program's by a relative error of at most 0.007.
Values may be sent and summed in bfloat16 or wider, within the bound.
No kernel may reach another device: no remote copies, remote signals or barrier semaphores. Data moves between devices by JAX's collectives and lax.ppermute only.
A program may use at most 128 MiB of HBM per device.

v0:
```python
import math
import jax
import jax.numpy as jnp
from jax import lax
from jax.sharding import Mesh
from jax.sharding import PartitionSpec as P

QK = 128
VD = 256
MAXLEN = 8192
lambda_start = 0.8 - 0.6 * math.exp(-3.3)
masked_score = -1e30


def locate(index, lengths):
    ends = jnp.cumsum(lengths)
    starts = ends - lengths
    segment = jnp.sum((ends[None, :] <= index[:, None]).astype(jnp.int32), axis=1)
    hit = jnp.arange(lengths.shape[0], dtype=jnp.int32)[None, :] == segment[:, None]
    begin = jnp.sum(jnp.where(hit, starts[None, :], 0), axis=1)
    return (segment, index - begin)


def rotate(proj, position):
    half = proj.shape[-1] // 2
    freq = 10000.0 ** (-jnp.arange(half, dtype=jnp.float32) / half)
    angle = position.astype(jnp.float32)[:, None] * freq[None, :]
    cosine = jnp.cos(angle)[:, None, None, :]
    sine = jnp.sin(angle)[:, None, None, :]
    front = proj[..., :half]
    back = proj[..., half:]
    return jnp.concatenate([front * cosine - back * sine, back * cosine + front * sine], axis=-1)


def swap_cores(value):
    return lax.ppermute(value, "core", [(0, 1), (1, 0)])


def on_device(tokens, norm_gain, w_query, w_key, w_value, w_out, lambdas, sub_gain, lengths):
    rows = tokens.shape[0]
    heads = w_query.shape[1] // (2 * QK)
    key_cols = heads * 2 * QK
    ys, zs, xs = (lax.axis_size("y"), lax.axis_size("z"), lax.axis_size("x"))
    chips = ys * zs * xs
    total = rows * 2 * chips
    core = lax.axis_index("core")
    chip = (lax.axis_index("y") * zs + lax.axis_index("z")) * xs + lax.axis_index("x")
    first = (chip * 2 + core) * rows
    local_index = first + jnp.arange(rows, dtype=jnp.int32)
    unused, pos_own = locate(local_index, lengths)
    xf = tokens.astype(jnp.float32)
    normed = (xf * lax.rsqrt(jnp.mean(xf * xf, axis=-1, keepdims=True) + 1e-06) * norm_gain).astype(
        jnp.bfloat16
    )
    keys = rotate(
        jnp.dot(normed, w_key, preferred_element_type=jnp.float32).reshape(rows, heads, 2, QK),
        pos_own,
    ).astype(jnp.bfloat16)
    values = jnp.dot(normed, w_value, preferred_element_type=jnp.float32).astype(jnp.bfloat16)
    key_flat = keys.reshape(rows, key_cols)
    lam = (
        jnp.exp(jnp.sum(lambdas[0] * lambdas[1], axis=-1))
        - jnp.exp(jnp.sum(lambdas[2] * lambdas[3], axis=-1))
        + lambda_start
    )
    scale = QK ** (-0.5)

    def head_kv(h):
        k_h = lax.dynamic_index_in_dim(keys, h, axis=1, keepdims=False).reshape(rows, 2 * QK)
        v_h = lax.dynamic_index_in_dim(values.reshape(rows, heads, VD), h, axis=1, keepdims=False)
        return jnp.concatenate([k_h, v_h], axis=1)

    def in_order(mine, theirs, first_is_mine):
        rows_each = mine.shape[0]
        both = jnp.zeros((2 * rows_each,) + mine.shape[1:], mine.dtype)
        both = lax.dynamic_update_slice_in_dim(
            both, mine, jnp.where(first_is_mine, 0, rows_each), axis=0
        )
        return lax.dynamic_update_slice_in_dim(
            both, theirs, jnp.where(first_is_mine, rows_each, 0), axis=0
        )

    span = 2 * rows
    z = lax.axis_index("z")
    kv_both = jnp.stack([head_kv(0), head_kv(1)], axis=1)
    halves = [
        lax.ppermute(kv_both[..., i * 2 * QK : (i + 1) * 2 * QK], "z", [(0, 1), (1, 0)])
        for i in range(2)
    ]
    kv_chips = in_order(kv_both, jnp.concatenate(halves, axis=-1), z == 0)
    mine = lax.dynamic_index_in_dim(kv_chips, core, axis=1, keepdims=False).reshape(2, rows, -1)
    theirs = swap_cores(
        lax.dynamic_index_in_dim(kv_chips, 1 - core, axis=1, keepdims=False)
    ).reshape(2, rows, -1)
    quad = jnp.zeros((2, span, mine.shape[-1]), mine.dtype)
    quad = lax.dynamic_update_slice_in_dim(quad, mine, core * rows, axis=1)
    quad = lax.dynamic_update_slice_in_dim(quad, theirs, (1 - core) * rows, axis=1)
    kv_quad = quad.reshape(2 * span, -1)
    kv_pair = lax.dynamic_index_in_dim(quad, z, axis=0, keepdims=False)
    gathered = lax.all_gather(kv_quad, ("y", "x"), axis=0, tiled=True)
    query = rotate(
        jnp.dot(normed, w_query, preferred_element_type=jnp.float32).reshape(rows, heads, 2, QK),
        pos_own,
    ).astype(jnp.bfloat16)
    q_pair = in_order(
        lax.dynamic_index_in_dim(query, core, axis=1, keepdims=False),
        swap_cores(lax.dynamic_index_in_dim(query, 1 - core, axis=1, keepdims=False)),
        core == 0,
    )
    reach = min(MAXLEN // span, chips - 1)
    window = reach * span
    base = chip * span
    first_chip = jnp.clip(chip - reach, 0, chips - reach)
    start = first_chip * span
    q_index = base + jnp.arange(span, dtype=jnp.int32)
    q_seg, unused = locate(q_index, lengths)

    def stats_of(kv_win, key_index, allowed):
        v_win = kv_win[:, 2 * QK :]
        stats = []
        for m in range(2):
            k_m = kv_win[:, m * QK : (m + 1) * QK]
            scores = (
                jnp.einsum("qd,kd->qk", q_pair[:, m, :], k_m, preferred_element_type=jnp.float32)
                * scale
            )
            scores = jnp.where(allowed, scores, masked_score)
            top = jnp.max(scores, axis=-1, keepdims=True)
            weights = jnp.where(allowed, jnp.exp(scores - top), 0.0)
            mass = jnp.sum(weights, axis=-1, keepdims=True)
            acc = jnp.dot(weights.astype(jnp.bfloat16), v_win, preferred_element_type=jnp.float32)
            stats.append((top, mass, acc))
        return stats

    local_allowed = (q_index[None, :] <= q_index[:, None]) & (q_seg[None, :] == q_seg[:, None])
    local_stats = stats_of(kv_pair, q_index, local_allowed)
    local_stats, gathered = lax.optimization_barrier((local_stats, gathered))
    c = first_chip + jnp.arange(reach, dtype=jnp.int32)
    slot = (c // (zs * xs) * xs + c % xs) * zs + c // xs % zs
    kv_window = jnp.take(gathered.reshape(chips, span, -1), slot, axis=0, mode="clip").reshape(
        window, -1
    )
    pieces = 2
    piece = window // pieces

    def part(p):
        key_index = start + p * piece + jnp.arange(piece, dtype=jnp.int32)
        k_seg, unused = locate(key_index, lengths)
        allowed = (key_index[None, :] < base) & (k_seg[None, :] == q_seg[:, None])
        return stats_of(kv_window[p * piece : (p + 1) * piece], key_index, allowed)

    all_stats = [local_stats] + [part(p) for p in range(pieces)]

    def attend(m):
        tops = [stats[m][0] for stats in all_stats]
        top = tops[0]
        for other in tops[1:]:
            top = jnp.maximum(top, other)
        acc = 0.0
        mass = 0.0
        for stats in all_stats:
            fade = jnp.exp(stats[m][0] - top)
            mass = mass + stats[m][1] * fade
            acc = acc + stats[m][2] * fade
        return acc / mass

    lam_h = lax.dynamic_index_in_dim(lam, core, keepdims=False)
    gain_h = lax.dynamic_index_in_dim(sub_gain, core, axis=0, keepdims=False)
    diff = attend(0) - lam_h * attend(1)
    head_out = (
        diff
        * lax.rsqrt(jnp.mean(diff * diff, axis=-1, keepdims=True) + 1e-05)
        * gain_h
        * (1.0 - lambda_start)
    ).astype(jnp.bfloat16)
    own_rows = lax.dynamic_slice_in_dim(head_out, core * rows, rows, axis=0)
    other_rows = swap_cores(lax.dynamic_slice_in_dim(head_out, (1 - core) * rows, rows, axis=0))
    merged = jnp.where(
        core == 0,
        jnp.concatenate([own_rows, other_rows], axis=1),
        jnp.concatenate([other_rows, own_rows], axis=1),
    )
    summed = lax.psum(
        jnp.dot(merged, w_out, preferred_element_type=jnp.float32).astype(jnp.bfloat16), "tp"
    ).astype(jnp.float32)
    hidden = (xf + summed).astype(jnp.bfloat16)
    return (hidden, key_flat, values)


def solution(mesh):
    req, tp = (mesh.shape["req"], mesh.shape["tp"])
    paired = Mesh(mesh.devices.reshape(req // 16, 2, 4, 2, tp), ("y", "z", "x", "core", "tp"))
    rows = ("y", "z", "x", "core")
    in_specs = (
        P(rows, None),
        P(),
        P(None, "tp"),
        P(None, "tp"),
        P(None, "tp"),
        P("tp", None),
        P(None, "tp", None),
        P("tp", None),
        P(),
    )
    out_specs = (P(rows, None), P(rows, "tp"), P(rows, "tp"))
    return jax.shard_map(
        on_device, mesh=paired, in_specs=in_specs, out_specs=out_specs, check_vma=False
    )
```

profile of v0, /device:TPU:1, one launch (start us, length us, event | category | flops | bytes accessed | tf_op | source)
XLA Modules:
  0.0 296.7 jit_solution(17206890886922927815)
XLA Ops:
  7.3 1.0 reduce-window.8
  9.1 1.5 fusion.16
  10.6 2.7 fusion.131
  14.2 0.8 multiply_subtract_fusion
  15.0 0.7 maximum_convert_fusion
  15.7 0.8 fusion.136
  16.6 2.7 convolution_convert_fusion.1
  20.4 0.9 copy.47
  21.5 0.8 fusion.103
  22.2 2.5 collective-permute-start.1
  24.8 5.1 %collective-permute-done.1 = bf16[256,2,256]{2,0,1:T(8,128)(2,1)S(1)} collective-permute-done((bf16[256,2,256]{2,0,1:T(8,128)(2,1)}, bf16[256,2,256]{2,0,1:T(8,128)(2,1)S(1)}, u32[]{:S(2)}, u32[]{:S(2)}) %collective-permute-start.1) | collective-permute-done | bytes 262176 | tf_op jit(solution)/shard_map/ppermute | solution.py:87
  30.0 5.5 %collective-permute-done.2 = bf16[256,2,256]{2,0,1:T(8,128)(2,1)} collective-permute-done((bf16[256,2,256]{2,0,1:T(8,128)(2,1)S(1)}, bf16[256,2,256]{2,0,1:T(8,128)(2,1)}, u32[]{:S(2)}, u32[]{:S(2)}) %collective-permute-start.2) | collective-permute-done | bytes 262176 | tf_op jit(solution)/shard_map/ppermute | solution.py:87
  35.5 1.0 maximum_dynamic-update-slice_fusion
  36.5 1.0 dynamic-slice_bitcast_fusion.1
  37.5 2.4 collective-permute-start.3
  40.0 1.1 constant_dynamic-update-slice_fusion.1
  41.1 0.7 collective-permute-done.3
  41.8 1.1 constant_dynamic-update-slice_fusion
  42.9 1.0 copy-done.1
  43.9 3.6 %fusion.133 = f32[256,512]{1,0:T(8,128)} fusion(bf16[2048,512]{1,0:T(8,128)(2,1)} %param.11, bf16[256,2048]{1,0:T(8,128)(2,1)} %param.9, f32[2048]{0:T(1024)S(1)} %copy-done.16, f32[256]{0:T(256)S(1)} %add_rsqrt_fusion.1), kind=kOutput, calls=%fused_computation.180 | convolution fusion | flops 538968064 | bytes 3679232 | tf_op jit(solution)/shard_map/dot_general | solution.py:102
  47.5 2.2 reshape.336
  49.7 2.0 add_convert_fusion
  51.7 0.7 fusion.113
  56.0 1.3 convert_reduce_fusion.2
  59.3 1.2 dynamic_slice.55
  60.4 0.9 convert_reduce_fusion.1
  61.3 1.6 constant_dynamic-update-slice_fusion.2
  63.0 1.3 fusion.139
  64.3 1.3 fusion.138
  66.6 1.4 fusion.97
  68.0 94.9 %all-gather.2.cloned.1.call-done = bf16[16384,512]{1,0:T(8,128)(2,1)} async-done(((bf16[1024,512]{1,0:T(8,128)(2,1)}), bf16[16384,512]{1,0:T(8,128)(2,1)}) %all-gather.2.cloned.1.call-update) | async-done | bytes 16777232 | tf_op jit(solution)/shard_map/all_gather | solution.py:100
  162.8 10.7 %gather_fusion = bf16[16,512,512]{2,1,0:T(8,128)(2,1)} fusion(bf16[32,512,512]{2,1,0:T(8,128)(2,1)} %bitcast.87, s32[1024]{0:T(1024)} %pad_clamp_fusion), kind=kCustom, calls=%fused_computation | custom fusion | bytes 16777280 | tf_op jit(solution)/shard_map/jit(_take)/gather | solution.py:140
  173.5 3.9 %fusion.135 = (bf16[8,512,512]{2,1,0:T(8,128)(2,1)S(1)}, bf16[8,512,512]{2,1,0:T(8,128)(2,1)S(1)}) fusion(bf16[16,512,512]{2,1,0:T(8,128)(2,1)} %gather_fusion), kind=kLoop, calls=%fused_computation.181 | loop fusion | bytes 16777216 | tf_op jit(solution)/shard_map/slice | solution.py:150
  177.4 2.4 fusion.142
  179.8 2.4 fusion.141
  182.2 4.6 %fusion.143 = (f32[512]{0:T(512)S(1)}, f32[512,4096]{1,0:T(8,128)}) fusion(bf16[4096,512]{1,0:T(8,128)(2,1)S(1)} %bitcast.92, bf16[512,2,128]{2,0,1:T(8,128)(2,1)S(1)} %copy-done.8, s32[512]{0:T(512)S(1)} %copy-done.9, s32[4096]{0:T(1024)S(1)} %get-tuple-element.28, pred[4096]{0:T(1024)(128)(4,1)S(1)} %copy-done.13), kind=kOutput, calls=%fused_computation.189 | convolution fusion | flops 547356160 | bytes 9592832 | tf_op jit(solution)/shard_map/qd,kd->qk/dot_general | solution.py:124
  186.8 3.6 %fusion.140 = (f32[512]{0:T(512)S(1)}, f32[512,4096]{1,0:T(8,128)S(1)}) fusion(bf16[4096,512]{1,0:T(8,128)(2,1)} %bitcast.93, bf16[512,2,128]{2,0,1:T(8,128)(2,1)S(1)} %copy-done.8, s32[512]{0:T(512)S(1)} %copy-done.9, s32[4096]{0:T(1024)S(1)} %get-tuple-element.28, pred[4096]{0:T(1024)(128)(4,1)S(1)} %copy-done.13), kind=kOutput, calls=%fused_computation.186 | convolution fusion | flops 547356160 | bytes 9592832 | tf_op jit(solution)/shard_map/qd,kd->qk/dot_general | solution.py:124
  190.4 11.0 %fusion.4 = (f32[512]{0:T(512)S(1)}, f32[512]{0:T(512)S(1)}, f32[512]{0:T(512)S(1)}, f32[512]{0:T(512)S(1)}) fusion(f32[512,4096]{1,0:T(8,128)S(1)} %get-tuple-element.64, f32[512]{0:T(512)S(1)} %get-tuple-element.63, s32[4096]{0:T(1024)S(1)} %get-tuple-element.27, s32[512]{0:T(512)S(1)} %copy-done.9, pred[4096]{0:T(1024)(128)(4,1)S(1)} %copy-done.12, ...), kind=kLoop, calls=%fused_computation.15 | loop fusion | flops 33552384 | bytes 33613824 | tf_op jit(solution)/shard_map/reduce_sum | solution.py:130
  201.4 5.6 %fusion.61 = f32[512,256]{1,0:T(8,128)S(1)} fusion(bf16[4096,512]{1,0:T(8,128)(2,1)} %bitcast.94, f32[512,4096]{1,0:T(8,128)} %get-tuple-element.68, f32[512]{0:T(512)S(1)} %get-tuple-element.67, s32[4096]{0:T(1024)S(1)} %get-tuple-element.28, s32[512]{0:T(512)S(1)} %copy-done.9, pred[4096]{0:T(1024)(128)(4,1)S(1)} %copy-done.13, f32[512]{0:T(512)S(1)} %bitcast.124), kind=kOutput, calls=%fused_computation.46 | convolution fusion | flops 1084358656 | bytes 11036672 | tf_op jit(solution)/shard_map/dot_general | solution.py:131
  207.1 3.9 %fusion.41 = f32[512,256]{1,0:T(8,128)S(1)} fusion(bf16[4096,512]{1,0:T(8,128)(2,1)} %bitcast.95, f32[512,4096]{1,0:T(8,128)S(1)} %get-tuple-element.62, f32[512]{0:T(512)S(1)} %get-tuple-element.61, s32[4096]{0:T(1024)S(1)} %get-tuple-element.28, s32[512]{0:T(512)S(1)} %copy-done.9, pred[4096]{0:T(1024)(128)(4,1)S(1)} %copy-done.13, f32[512]{0:T(512)S(1)} %bitcast.123), kind=kOutput, calls=%fused_computation.42 | convolution fusion | flops 1084358656 | bytes 11036672 | tf_op jit(solution)/shard_map/dot_general | solution.py:131
  211.1 2.4 fusion.85
  213.4 3.1 %multiply_reduce_fusion = (f32[512]{0:T(512)S(1)}, f32[512,256]{1,0:T(8,128)S(1)}) fusion(f32[512,256]{1,0:T(8,128)S(1)} %fusion.85, f32[512]{0:T(512)S(1)} %bitcast.117, f32[512,256]{1,0:T(8,128)S(1)} %fusion.61, f32[512]{0:T(512)S(1)} %bitcast.119, bf16[4096,512]{1,0:T(8,128)(2,1)S(1)} %bitcast.91, f32[512,4096]{1,0:T(8,128)S(1)} %get-tuple-element.64, ...), kind=kOutput, calls=%fused_computation.74 | convolution fusion | flops 1085406720 | bytes 12615684 | tf_op jit(solution)/shard_map/dot_general | solution.py:131
  216.7 0.8 collective-permute-start.4
  217.5 1.0 collective-permute-done.4
  218.5 1.7 convolution_convert_fusion
  220.2 0.8 convert_element_type.86
  221.0 66.2 %all-reduce.2.cloned.1.call-done = bf16[256,2048]{1,0:T(8,128)(2,1)} async-done(((bf16[256,2048]{1,0:T(8,128)(2,1)}), bf16[256,2048]{1,0:T(8,128)(2,1)}) %all-reduce.2.cloned.1.call-update) | async-done | bytes 1048592 | tf_op jit(solution)/shard_map/psum | solution.py:183
  287.2 2.6 fusion.19
  (80 shorter events, 10.1 us)
Async XLA Ops:
  7.2 211.3 %copy-start = (bf16[512,2048]{1,0:T(8,128)(2,1)S(1)}, bf16[512,2048]{1,0:T(8,128)(2,1)}, u32[]{:S(2)}) copy-start(bf16[512,2048]{1,0:T(8,128)(2,1)} %param.14) | copy-start | bytes 6291460
  7.2 155.7 %all-gather.2.cloned.1.call-start = ((), (), s32[]{:S(2)}) async-start(), calls=%async_computation | async-start | bytes 17825792 | tf_op jit(solution)/shard_map/all_gather | solution.py:100
  8.2 2.4 copy-start.14
  10.6 6.0 %copy-start.16 = (f32[2048]{0:T(1024)S(1)}, f32[2048]{0:T(1024)}, u32[]{:S(2)}) copy-start(f32[2048]{0:T(1024)} %param.10) | copy-start | bytes 24580
  14.2 5.9 %copy-start.5 = (f32[256,64]{1,0:T(8,128)}, f32[256,64]{1,0:T(8,128)S(1)}, u32[]{:S(2)}) copy-start(f32[256,64]{1,0:T(8,128)S(1)} %get-tuple-element.56) | copy-start | bytes 196612
  19.3 0.7 copy-start.6
  22.2 7.8 %collective-permute-start.1 = (bf16[256,2,256]{2,0,1:T(8,128)(2,1)}, bf16[256,2,256]{2,0,1:T(8,128)(2,1)S(1)}, u32[]{:S(2)}, u32[]{:S(2)}) collective-permute-start(bf16[256,2,256]{2,0,1:T(8,128)(2,1)} %get-tuple-element.47), channel_id=1, source_target_pairs={{0,32},{32,0},{1,33},{33,1},{2,34},{34,2},{3,35},{35,3},{4,36},{36... | collective-permute-start | bytes 786440 | tf_op jit(solution)/shard_map/ppermute | solution.py:87
  24.7 10.8 %collective-permute-start.2 = (bf16[256,2,256]{2,0,1:T(8,128)(2,1)S(1)}, bf16[256,2,256]{2,0,1:T(8,128)(2,1)}, u32[]{:S(2)}, u32[]{:S(2)}) collective-permute-start(bf16[256,2,256]{2,0,1:T(8,128)(2,1)S(1)} %get-tuple-element.48), channel_id=1, source_target_pairs={{0,32},{32,0},{1,33},{33,1},{2,34},{34,2},{3,35},{35,3},{4,36},{36... | collective-permute-start | bytes 786440 | tf_op jit(solution)/shard_map/ppermute | solution.py:87
  37.5 4.3 %collective-permute-start.3 = (bf16[512,512]{1,0:T(8,128)(2,1)}, bf16[512,512]{1,0:T(8,128)(2,1)}, u32[]{:S(2)}, u32[]{:S(2)}) collective-permute-start(bf16[512,512]{1,0:T(8,128)(2,1)} %get-tuple-element.39), channel_id=1, source_target_pairs={{0,4},{4,0},{1,5},{5,1},{2,6},{6,2},{3,7},{7,3},{8,12},{12,8},{9,1... | collective-permute-start | bytes 1572872 | tf_op jit(solution)/shard_map/ppermute | solution.py:36
  42.9 1.0 copy-start.1
  43.9 11.4 %copy-start.15 = (f32[4,2,128]{2,1,0:T(2,128)S(1)}, f32[4,2,128]{2,1,0:T(2,128)}, u32[]{:S(2)}) copy-start(f32[4,2,128]{2,1,0:T(2,128)} %param.15) | copy-start | bytes 12292
  43.9 19.1 %copy-start.2 = (bf16[2,512,512]{2,1,0:T(8,128)(2,1)S(1)}, bf16[2,512,512]{2,1,0:T(8,128)(2,1)}, u32[]{:S(2)}) copy-start(bf16[2,512,512]{2,1,0:T(8,128)(2,1)} %copy-done.1) | copy-start | bytes 3145732
  43.9 243.3 %all-reduce.2.cloned.1.call-start = ((), (), s32[]{:S(2)}) async-start(), calls=%async_computation.1 | async-start | bytes 2097152 | tf_op jit(solution)/shard_map/psum | solution.py:183
  53.1 8.3 %collective-permute-start = (bf16[256,2,128]{2,0,1:T(8,128)(2,1)}, bf16[256,2,128]{2,0,1:T(8,128)(2,1)}, u32[]{:S(2)}, u32[]{:S(2)}) collective-permute-start(bf16[256,2,128]{2,0,1:T(8,128)(2,1)} %bitcast.85), channel_id=1, source_target_pairs={{0,4},{4,0},{1,5},{5,1},{2,6},{6,2},{3,7},{7,3},{8,12},{12,8},{9,1... | collective-permute-start | bytes 393224 | tf_op jit(solution)/shard_map/ppermute | solution.py:36
  53.5 4.3 %copy-start.10 = (s32[512]{0:T(512)}, s32[512]{0:T(512)S(1)}, u32[]{:S(2)}) copy-start(s32[512]{0:T(512)S(1)} %iota_add_fusion.2) | copy-start | bytes 6148
  57.9 0.7 copy-start.7
  58.6 7.0 %copy-start.9 = (s32[512]{0:T(512)S(1)}, s32[512]{0:T(512)}, u32[]{:S(2)}) copy-start(s32[512]{0:T(512)} %convert_reduce_fusion.2) | copy-start | bytes 6148
  58.6 7.0 %copy-start.11 = (s32[512]{0:T(512)S(1)}, s32[512]{0:T(512)}, u32[]{:S(2)}) copy-start(s32[512]{0:T(512)} %copy-done.10) | copy-start | bytes 6148
  173.5 3.9 %copy-start.8 = (bf16[512,2,128]{2,0,1:T(8,128)(2,1)S(1)}, bf16[512,2,128]{2,0,1:T(8,128)(2,1)}, u32[]{:S(2)}) copy-start(bf16[512,2,128]{2,0,1:T(8,128)(2,1)} %constant_dynamic-update-slice_fusion.2) | copy-start | bytes 786436
  173.5 3.9 %copy-start.12 = (pred[4096]{0:T(1024)(128)(4,1)S(1)}, pred[4096]{0:T(1024)(128)(4,1)}, u32[]{:S(2)}) copy-start(pred[4096]{0:T(1024)(128)(4,1)} %broadcast_compare_fusion.1) | copy-start | bytes 12292
  177.4 4.8 %copy-start.4 = (bf16[8,512,512]{2,1,0:T(8,128)(2,1)}, bf16[8,512,512]{2,1,0:T(8,128)(2,1)S(1)}, u32[]{:S(2)}) copy-start(bf16[8,512,512]{2,1,0:T(8,128)(2,1)S(1)} %get-tuple-element.38) | copy-start | bytes 12582916
  179.8 2.4 copy-start.13
  207.1 4.0 %copy-start.17 = (f32[512,256]{1,0:T(8,128)S(1)}, f32[512,256]{1,0:T(8,128)}, u32[]{:S(2)}) copy-start(f32[512,256]{1,0:T(8,128)} %fusion.97) | copy-start | bytes 1572868
  216.5 70.7 %copy-start.3 = (bf16[256,2048]{1,0:T(8,128)(2,1)S(1)}, bf16[256,2048]{1,0:T(8,128)(2,1)}, u32[]{:S(2)}) copy-start(bf16[256,2048]{1,0:T(8,128)(2,1)} %param.9) | copy-start | bytes 3145732
  216.7 1.8 collective-permute-start.4
Sparse Core Ops, SparseCore 0:
  44.0 118.7 all-gather.1
  220.3 66.8 all-reduce.1
where the time goes:
time: 297 us
  waiting for transfers between devices  173 us (58%)
  matrix products  43.2 us (15%)
  local copies, waits for them, and re-layouts  30.1 us (10%)
  other arithmetic  29.3 us (10%)
  between operations  14.5 us (5%)
  starting transfers between devices  6.13 us (2%)
    all_gather x1, waiting for transfers between devices, on_device(): gathered = lax.all_gather(kv_quad, ('y', 'x'), axis=0, tiled=True)  94.9 us
    psum x1, waiting for transfers between devices, on_device(): lax.psum(jnp.dot(merged, w_out, preferred_element_type=jnp.float32).astyp...  66.2 us
    dot_general x6, matrix products, stats_of(): jnp.dot(weights.astype(jnp.bfloat16), v_win, preferred_element_type=jnp.f...  17 us
    dot_general x6, matrix products, stats_of(): jnp.einsum('qd,kd->qk', q_pair[:, m, :], k_m, preferred_element_type=jnp....  15.6 us
    reduce_sum x2, other arithmetic, stats_of(): mass = jnp.sum(weights, axis=-1, keepdims=True)  11.4 us
    gather x1, local copies, waits for them, and re-layouts, on_device(): jnp.take(gathered.reshape(chips, span, -1), slot, axis=0, mode='clip')  10.7 us
    ppermute x2, waiting for transfers between devices, on_device(): lax.ppermute(kv_both[..., i * 2 * QK:(i + 1) * 2 * QK], 'z', [(0, 1), (1,...  10.6 us
  transfers between devices with their start and end apart: 7, of which 6 were waited for; matrix products, arithmetic and copies ran while one was open for 8% of the time, Pallas kernels for 0%

commit v1 on v0

--- a/solution.py
+++ b/solution.py
@@ -180,8 +180,11 @@
         jnp.concatenate([own_rows, other_rows], axis=1),
         jnp.concatenate([other_rows, own_rows], axis=1),
     )
-    summed = lax.psum(
-        jnp.dot(merged, w_out, preferred_element_type=jnp.float32).astype(jnp.bfloat16), "tp"
+    summed = jnp.sum(
+        lax.all_gather(
+            jnp.dot(merged, w_out, preferred_element_type=jnp.float32).astype(jnp.bfloat16), "tp"
+        ),
+        axis=0,
     ).astype(jnp.float32)
     hidden = (xf + summed).astype(jnp.bfloat16)
     return (hidden, key_flat, values)

time: 297 us -> 320 us (1.077)
  the two profiles are of different devices: /device:TPU:1 before, /device:TPU:37 now
where the time goes in v1:
time: 320 us; the launch traced here: 319 us
  waiting for transfers between devices  194 us (61%)
  matrix products  43.2 us (14%)
  other arithmetic  33.5 us (10%)
  local copies, waits for them, and re-layouts  30.1 us (9%)
  between operations  14.5 us (5%)
  starting transfers between devices  4.22 us (1%)
    all_gather x1, waiting for transfers between devices, on_device(): gathered = lax.all_gather(kv_quad, ('y', 'x'), axis=0, tiled=True)  94.6 us
    all_gather x1, waiting for transfers between devices, on_device(): lax.all_gather(jnp.dot(merged, w_out, preferred_element_type=jnp.float32)...  85.7 us
    dot_general x6, matrix products, stats_of(): jnp.dot(weights.astype(jnp.bfloat16), v_win, preferred_element_type=jnp.f...  17 us
    dot_general x6, matrix products, stats_of(): jnp.einsum('qd,kd->qk', q_pair[:, m, :], k_m, preferred_element_type=jnp....  15.6 us
    ppermute x2, waiting for transfers between devices, on_device(): lax.ppermute(kv_both[..., i * 2 * QK:(i + 1) * 2 * QK], 'z', [(0, 1), (1,...  11.5 us
    reduce_sum x2, other arithmetic, stats_of(): mass = jnp.sum(weights, axis=-1, keepdims=True)  11.4 us
    gather x1, local copies, waits for them, and re-layouts, on_device(): jnp.take(gathered.reshape(chips, span, -1), slot, axis=0, mode='clip')  10.7 us
  transfers between devices with their start and end apart: 7, of which 6 were waited for; matrix products, arithmetic and copies ran while one was open for 8% of the time, Pallas kernels for 0%

profile of v1, /device:TPU:37, one launch (start us, length us, event | category | flops | bytes accessed | tf_op | source)
XLA Modules:
  0.0 319.2 jit_solution(12914185535965978246)
XLA Ops:
  7.3 1.0 reduce-window.8
  9.1 1.5 fusion.16
  10.6 2.7 fusion.131
  14.2 0.8 multiply_subtract_fusion
  15.0 0.7 maximum_convert_fusion
  15.7 0.8 fusion.136
  16.6 2.7 convolution_convert_fusion.1
  20.4 0.9 copy.47
  21.5 0.8 fusion.103
  22.2 1.5 collective-permute-start.2
  23.8 5.8 %collective-permute-done.1 = bf16[256,2,256]{2,0,1:T(8,128)(2,1)S(1)} collective-permute-done((bf16[256,2,256]{2,0,1:T(8,128)(2,1)}, bf16[256,2,256]{2,0,1:T(8,128)(2,1)S(1)}, u32[]{:S(2)}, u32[]{:S(2)}) %collective-permute-start.1) | collective-permute-done | bytes 262176 | tf_op jit(solution)/shard_map/ppermute | solution.py:87
  29.6 5.7 %collective-permute-done.2 = bf16[256,2,256]{2,0,1:T(8,128)(2,1)} collective-permute-done((bf16[256,2,256]{2,0,1:T(8,128)(2,1)S(1)}, bf16[256,2,256]{2,0,1:T(8,128)(2,1)}, u32[]{:S(2)}, u32[]{:S(2)}) %collective-permute-start.2) | collective-permute-done | bytes 262176 | tf_op jit(solution)/shard_map/ppermute | solution.py:87
  35.3 1.0 maximum_dynamic-update-slice_fusion
  36.3 1.0 dynamic-slice_bitcast_fusion.1
  37.4 1.5 collective-permute-start.3
  39.0 1.1 constant_dynamic-update-slice_fusion.1
  40.8 1.1 constant_dynamic-update-slice_fusion
  41.9 1.0 copy-done.1
  43.0 3.6 %fusion.133 = f32[256,512]{1,0:T(8,128)} fusion(bf16[2048,512]{1,0:T(8,128)(2,1)} %param.11, bf16[256,2048]{1,0:T(8,128)(2,1)} %param.9, f32[2048]{0:T(1024)S(1)} %copy-done.16, f32[256]{0:T(256)S(1)} %add_rsqrt_fusion.1), kind=kOutput, calls=%fused_computation.180 | convolution fusion | flops 538968064 | bytes 3679232 | tf_op jit(solution)/shard_map/dot_general | solution.py:102
  46.5 2.2 reshape.336
  48.7 2.0 add_convert_fusion
  50.7 0.7 fusion.113
  55.0 1.3 convert_reduce_fusion.2
  58.3 1.2 dynamic_slice.55
  59.5 0.9 convert_reduce_fusion.1
  60.3 1.6 constant_dynamic-update-slice_fusion.2
  62.0 1.3 fusion.139
  63.3 1.3 fusion.138
  65.6 1.4 fusion.97
  67.0 94.6 %all-gather.4.cloned.1.call-done = bf16[16384,512]{1,0:T(8,128)(2,1)} async-done(((bf16[1024,512]{1,0:T(8,128)(2,1)}), bf16[16384,512]{1,0:T(8,128)(2,1)}) %all-gather.4.cloned.1.call-update) | async-done | bytes 16777232 | tf_op jit(solution)/shard_map/all_gather | solution.py:100
  161.6 10.7 %gather_fusion = bf16[16,512,512]{2,1,0:T(8,128)(2,1)} fusion(bf16[32,512,512]{2,1,0:T(8,128)(2,1)} %bitcast.88, s32[1024]{0:T(1024)} %pad_clamp_fusion), kind=kCustom, calls=%fused_computation | custom fusion | bytes 16777280 | tf_op jit(solution)/shard_map/jit(_take)/gather | solution.py:140
  172.3 3.9 %fusion.135 = (bf16[8,512,512]{2,1,0:T(8,128)(2,1)S(1)}, bf16[8,512,512]{2,1,0:T(8,128)(2,1)S(1)}) fusion(bf16[16,512,512]{2,1,0:T(8,128)(2,1)} %gather_fusion), kind=kLoop, calls=%fused_computation.181 | loop fusion | bytes 16777216 | tf_op jit(solution)/shard_map/slice | solution.py:150
  176.2 2.4 fusion.142
  178.6 2.4 fusion.141
  180.9 4.6 %fusion.143 = (f32[512]{0:T(512)S(1)}, f32[512,4096]{1,0:T(8,128)}) fusion(bf16[4096,512]{1,0:T(8,128)(2,1)S(1)} %bitcast.94, bf16[512,2,128]{2,0,1:T(8,128)(2,1)S(1)} %copy-done.8, s32[512]{0:T(512)S(1)} %copy-done.9, s32[4096]{0:T(1024)S(1)} %get-tuple-element.28, pred[4096]{0:T(1024)(128)(4,1)S(1)} %copy-done.13), kind=kOutput, calls=%fused_computation.189 | convolution fusion | flops 547356160 | bytes 9592832 | tf_op jit(solution)/shard_map/qd,kd->qk/dot_general | solution.py:124
  185.6 3.6 %fusion.140 = (f32[512]{0:T(512)S(1)}, f32[512,4096]{1,0:T(8,128)S(1)}) fusion(bf16[4096,512]{1,0:T(8,128)(2,1)} %bitcast.95, bf16[512,2,128]{2,0,1:T(8,128)(2,1)S(1)} %copy-done.8, s32[512]{0:T(512)S(1)} %copy-done.9, s32[4096]{0:T(1024)S(1)} %get-tuple-element.28, pred[4096]{0:T(1024)(128)(4,1)S(1)} %copy-done.13), kind=kOutput, calls=%fused_computation.186 | convolution fusion | flops 547356160 | bytes 9592832 | tf_op jit(solution)/shard_map/qd,kd->qk/dot_general | solution.py:124
  189.2 11.0 %fusion.4 = (f32[512]{0:T(512)S(1)}, f32[512]{0:T(512)S(1)}, f32[512]{0:T(512)S(1)}, f32[512]{0:T(512)S(1)}) fusion(f32[512,4096]{1,0:T(8,128)S(1)} %get-tuple-element.64, f32[512]{0:T(512)S(1)} %get-tuple-element.63, s32[4096]{0:T(1024)S(1)} %get-tuple-element.27, s32[512]{0:T(512)S(1)} %copy-done.9, pred[4096]{0:T(1024)(128)(4,1)S(1)} %copy-done.12, ...), kind=kLoop, calls=%fused_computation.15 | loop fusion | flops 33552384 | bytes 33613824 | tf_op jit(solution)/shard_map/reduce_sum | solution.py:130
  200.1 5.6 %fusion.61 = f32[512,256]{1,0:T(8,128)S(1)} fusion(bf16[4096,512]{1,0:T(8,128)(2,1)} %bitcast.96, f32[512,4096]{1,0:T(8,128)} %get-tuple-element.68, f32[512]{0:T(512)S(1)} %get-tuple-element.67, s32[4096]{0:T(1024)S(1)} %get-tuple-element.28, s32[512]{0:T(512)S(1)} %copy-done.9, pred[4096]{0:T(1024)(128)(4,1)S(1)} %copy-done.13, f32[512]{0:T(512)S(1)} %bitcast.126), kind=kOutput, calls=%fused_computation.46 | convolution fusion | flops 1084358656 | bytes 11036672 | tf_op jit(solution)/shard_map/dot_general | solution.py:131
  205.8 3.9 %fusion.41 = f32[512,256]{1,0:T(8,128)S(1)} fusion(bf16[4096,512]{1,0:T(8,128)(2,1)} %bitcast.97, f32[512,4096]{1,0:T(8,128)S(1)} %get-tuple-element.62, f32[512]{0:T(512)S(1)} %get-tuple-element.61, s32[4096]{0:T(1024)S(1)} %get-tuple-element.28, s32[512]{0:T(512)S(1)} %copy-done.9, pred[4096]{0:T(1024)(128)(4,1)S(1)} %copy-done.13, f32[512]{0:T(512)S(1)} %bitcast.125), kind=kOutput, calls=%fused_computation.42 | convolution fusion | flops 1084358656 | bytes 11036672 | tf_op jit(solution)/shard_map/dot_general | solution.py:131
  209.8 2.4 fusion.85
  212.2 3.1 multiply_reduce_fusion
  215.5 0.8 collective-permute-start.4
  216.2 1.0 collective-permute-done.4
  217.2 1.7 convolution_convert_fusion
  219.0 0.8 convert_element_type.88
  219.8 85.7 %all-gather.6.cloned.1.call-done = bf16[1024,2048]{1,0:T(8,128)(2,1)} async-done(((bf16[256,2048]{1,0:T(8,128)(2,1)}), bf16[1024,2048]{1,0:T(8,128)(2,1)}) %all-gather.6.cloned.1.call-update) | async-done | bytes 4194320 | tf_op jit(solution)/shard_map/all_gather | solution.py:184
  305.5 4.2 %reduce_sum.162 = bf16[256,2048]{1,0:T(8,128)(2,1)} reduce(bf16[4,256,2048]{2,1,0:T(8,128)(2,1)} %bitcast.89, bf16[]{:T(256)} %constant.140.clone.1), dimensions={0}, to_apply=%region_22.23 | reduce | flops 1572864 | bytes 5242882 | tf_op jit(solution)/shard_map/reduce_sum | solution.py:183
  309.7 2.6 fusion.19
  (81 shorter events, 10.9 us)
Async XLA Ops:
  7.2 210.1 %copy-start = (bf16[512,2048]{1,0:T(8,128)(2,1)S(1)}, bf16[512,2048]{1,0:T(8,128)(2,1)}, u32[]{:S(2)}) copy-start(bf16[512,2048]{1,0:T(8,128)(2,1)} %param.14) | copy-start | bytes 6291460
  7.2 154.4 %all-gather.4.cloned.1.call-start = ((), (), s32[]{:S(2)}) async-start(), calls=%async_computation | async-start | bytes 17825792 | tf_op jit(solution)/shard_map/all_gather | solution.py:100
  8.2 2.4 copy-start.14
  10.6 6.0 %copy-start.16 = (f32[2048]{0:T(1024)S(1)}, f32[2048]{0:T(1024)}, u32[]{:S(2)}) copy-start(f32[2048]{0:T(1024)} %param.10) | copy-start | bytes 24580
  14.2 5.9 %copy-start.5 = (f32[256,64]{1,0:T(8,128)}, f32[256,64]{1,0:T(8,128)S(1)}, u32[]{:S(2)}) copy-start(f32[256,64]{1,0:T(8,128)S(1)} %get-tuple-element.56) | copy-start | bytes 196612
  19.3 0.7 copy-start.6
  22.2 7.4 %collective-permute-start.1 = (bf16[256,2,256]{2,0,1:T(8,128)(2,1)}, bf16[256,2,256]{2,0,1:T(8,128)(2,1)S(1)}, u32[]{:S(2)}, u32[]{:S(2)}) collective-permute-start(bf16[256,2,256]{2,0,1:T(8,128)(2,1)} %get-tuple-element.47), channel_id=1, source_target_pairs={{0,32},{32,0},{1,33},{33,1},{2,34},{34,2},{3,35},{35,3},{4,36},{36... | collective-permute-start | bytes 786440 | tf_op jit(solution)/shard_map/ppermute | solution.py:87
  22.2 13.1 %collective-permute-start.2 = (bf16[256,2,256]{2,0,1:T(8,128)(2,1)S(1)}, bf16[256,2,256]{2,0,1:T(8,128)(2,1)}, u32[]{:S(2)}, u32[]{:S(2)}) collective-permute-start(bf16[256,2,256]{2,0,1:T(8,128)(2,1)S(1)} %get-tuple-element.48), channel_id=1, source_target_pairs={{0,32},{32,0},{1,33},{33,1},{2,34},{34,2},{3,35},{35,3},{4,36},{36... | collective-permute-start | bytes 786440 | tf_op jit(solution)/shard_map/ppermute | solution.py:87
  37.4 3.4 %collective-permute-start.3 = (bf16[512,512]{1,0:T(8,128)(2,1)}, bf16[512,512]{1,0:T(8,128)(2,1)}, u32[]{:S(2)}, u32[]{:S(2)}) collective-permute-start(bf16[512,512]{1,0:T(8,128)(2,1)} %get-tuple-element.39), channel_id=1, source_target_pairs={{0,4},{4,0},{1,5},{5,1},{2,6},{6,2},{3,7},{7,3},{8,12},{12,8},{9,1... | collective-permute-start | bytes 1572872 | tf_op jit(solution)/shard_map/ppermute | solution.py:36
  41.9 1.0 copy-start.1
  42.9 11.4 %copy-start.15 = (f32[4,2,128]{2,1,0:T(2,128)S(1)}, f32[4,2,128]{2,1,0:T(2,128)}, u32[]{:S(2)}) copy-start(f32[4,2,128]{2,1,0:T(2,128)} %param.15) | copy-start | bytes 12292
  42.9 19.1 %copy-start.2 = (bf16[2,512,512]{2,1,0:T(8,128)(2,1)S(1)}, bf16[2,512,512]{2,1,0:T(8,128)(2,1)}, u32[]{:S(2)}) copy-start(bf16[2,512,512]{2,1,0:T(8,128)(2,1)} %copy-done.1) | copy-start | bytes 3145732
  42.9 262.6 %all-gather.6.cloned.1.call-start = ((), (), s32[]{:S(2)}) async-start(), calls=%async_computation.1 | async-start | bytes 5242880 | tf_op jit(solution)/shard_map/all_gather | solution.py:184
  52.1 8.3 %collective-permute-start = (bf16[256,2,128]{2,0,1:T(8,128)(2,1)}, bf16[256,2,128]{2,0,1:T(8,128)(2,1)}, u32[]{:S(2)}, u32[]{:S(2)}) collective-permute-start(bf16[256,2,128]{2,0,1:T(8,128)(2,1)} %bitcast.86), channel_id=1, source_target_pairs={{0,4},{4,0},{1,5},{5,1},{2,6},{6,2},{3,7},{7,3},{8,12},{12,8},{9,1... | collective-permute-start | bytes 393224 | tf_op jit(solution)/shard_map/ppermute | solution.py:36
  52.5 4.3 %copy-start.10 = (s32[512]{0:T(512)}, s32[512]{0:T(512)S(1)}, u32[]{:S(2)}) copy-start(s32[512]{0:T(512)S(1)} %iota_add_fusion.2) | copy-start | bytes 6148
  56.9 0.7 copy-start.7
  57.6 7.0 %copy-start.9 = (s32[512]{0:T(512)S(1)}, s32[512]{0:T(512)}, u32[]{:S(2)}) copy-start(s32[512]{0:T(512)} %convert_reduce_fusion.2) | copy-start | bytes 6148
  57.6 7.0 %copy-start.11 = (s32[512]{0:T(512)S(1)}, s32[512]{0:T(512)}, u32[]{:S(2)}) copy-start(s32[512]{0:T(512)} %copy-done.10) | copy-start | bytes 6148
  172.2 3.9 %copy-start.8 = (bf16[512,2,128]{2,0,1:T(8,128)(2,1)S(1)}, bf16[512,2,128]{2,0,1:T(8,128)(2,1)}, u32[]{:S(2)}) copy-start(bf16[512,2,128]{2,0,1:T(8,128)(2,1)} %constant_dynamic-update-slice_fusion.2) | copy-start | bytes 786436
  172.3 3.9 %copy-start.12 = (pred[4096]{0:T(1024)(128)(4,1)S(1)}, pred[4096]{0:T(1024)(128)(4,1)}, u32[]{:S(2)}) copy-start(pred[4096]{0:T(1024)(128)(4,1)} %broadcast_compare_fusion.1) | copy-start | bytes 12292
  176.1 4.8 %copy-start.4 = (bf16[8,512,512]{2,1,0:T(8,128)(2,1)}, bf16[8,512,512]{2,1,0:T(8,128)(2,1)S(1)}, u32[]{:S(2)}) copy-start(bf16[8,512,512]{2,1,0:T(8,128)(2,1)S(1)} %get-tuple-element.38) | copy-start | bytes 12582916
  178.5 2.4 copy-start.13
  205.8 4.0 %copy-start.17 = (f32[512,256]{1,0:T(8,128)S(1)}, f32[512,256]{1,0:T(8,128)}, u32[]{:S(2)}) copy-start(f32[512,256]{1,0:T(8,128)} %fusion.97) | copy-start | bytes 1572868
  215.5 1.7 collective-permute-start.4
  218.9 90.8 %copy-start.3 = (bf16[256,2048]{1,0:T(8,128)(2,1)S(1)}, bf16[256,2048]{1,0:T(8,128)(2,1)}, u32[]{:S(2)}) copy-start(bf16[256,2048]{1,0:T(8,128)(2,1)} %param.9) | copy-start | bytes 3145732
Sparse Core Ops, SparseCore 0:
  43.0 118.5 all-gather.3
  219.1 86.3 all-gather.5
